TPU v7x, 32 devices: a whole 2x2x4 slice. The times are simulated.
32 devices in a mesh: ctx: 8 (over y, x, core), mp: 4 (over z).
Axes of the slice: x: 2, y: 2, z: 4, core: 2. Of those that a mesh axis runs over, the one named last changes fastest.
Arguments:
- cotangent: bfloat16 [1536, 8192], P('ctx', 'mp'), may hold values from -6 to 6
- out_weight: bfloat16 [8192, 8192], P('mp', 'ctx'), may hold values from -0.0625 to 0.0625
- query_act: bfloat16 [1536, 8192], P('ctx', 'mp'), may hold values from -6 to 6
- key_act: bfloat16 [1536, 8192], P('ctx', 'mp'), may hold values from -6 to 6
- value_act: bfloat16 [1536, 8192], P('ctx', 'mp'), may hold values from -6 to 6
- filters: float32 [512, 128], replicated, may hold values from -0.5 to 0.5
Outputs:
- grad_query: bfloat16 [1536, 8192], P('ctx', 'mp')
- grad_key: bfloat16 [1536, 8192], P('ctx', 'mp')
- grad_value: bfloat16 [1536, 8192], P('ctx', 'mp')
- grad_filters: float32 [512, 128], replicated
All inputs are finite; a program needn't handle non-finite values.
Results may differ from a plain program's by a relative error of at most 0.0051.
Values may be sent and summed in bfloat16 or wider, within the bound.
No kernel may reach another device: no remote copies, remote signals or barrier semaphores. Data moves between devices by JAX's collectives and lax.ppermute only.
A program may use at most 128 MiB of HBM per device.

v0:
```python
import jax
import jax.numpy as jnp
from jax import lax
from jax.sharding import PartitionSpec as P


def contract(left, right):
    return lax.dot_general(
        left, right, (((1,), (1,)), ((), ())), preferred_element_type=jnp.float32
    )


def toeplitz(seq, block, width):
    groups = seq.shape[0]
    flat = jnp.tile(seq, (1, block))[:, : block * width]
    return flat.reshape(groups, block, width)


def split_bf16(x):
    hi = x.astype(jnp.bfloat16)
    lo = (x - hi.astype(jnp.float32)).astype(jnp.bfloat16)
    return (hi, lo)


def windows(x, tiles, block, width):
    return jnp.stack([x[k * block : k * block + width] for k in range(tiles)])


def filter_apply(mats, wins, groups, per_group):
    tiles, width, chans = wins.shape
    w4 = wins.reshape(tiles, width, groups, per_group)
    total = None
    for m in mats:
        part = jnp.einsum("gij,kjgc->kigc", m, w4, preferred_element_type=jnp.float32)
        total = part if total is None else total + part
    block = mats[0].shape[1]
    return total.reshape(tiles * block, chans)


def body(cotangent, out_weight, query_act, key_act, value_act, filters):
    rows, chans = cotangent.shape
    groups, flen = filters.shape
    ctx_count = lax.axis_size("ctx")
    mp_count = lax.axis_size("mp")
    per_group = chans * mp_count // groups
    local_groups = chans // per_group
    halo = flen
    block = 64 if rows % 64 == 0 else rows
    tiles = rows // block
    width = block + halo
    panel = lax.all_gather(out_weight, "ctx", axis=1, tiled=True)
    grad_mixed = contract(lax.all_gather(cotangent, "mp", axis=1, tiled=True), panel)
    product = (key_act.astype(jnp.float32) * value_act.astype(jnp.float32)).astype(jnp.bfloat16)
    grad_conv = (grad_mixed * query_act.astype(jnp.float32)).astype(jnp.bfloat16)
    fwd = [(k, k + 1) for k in range(ctx_count - 1)]
    bwd = [(k + 1, k) for k in range(ctx_count - 1)]
    prev_tail = lax.ppermute(product[rows - halo :], "ctx", fwd)
    next_head = lax.ppermute(grad_conv[:halo], "ctx", bwd)
    taps = lax.dynamic_slice_in_dim(filters, lax.axis_index("mp") * local_groups, local_groups, 0)
    pad = jnp.zeros((local_groups, width + 1 - flen - 1), jnp.float32)
    one = jnp.zeros((local_groups, 1), jnp.float32)
    seq_causal = jnp.concatenate([one, taps[:, ::-1], pad], 1)
    seq_anti = jnp.concatenate([taps, pad, one], 1)
    mats_causal = split_bf16(toeplitz(seq_causal, block, width))
    mats_anti = split_bf16(toeplitz(seq_anti, block, width))
    widened = jnp.concatenate([prev_tail, product], 0)
    trailing = jnp.concatenate([grad_conv, next_head], 0)
    win_prod = windows(widened, tiles, block, width)
    win_grad = windows(trailing, tiles, block, width)
    mixed = filter_apply(mats_causal, win_prod, local_groups, per_group)
    grad_product = filter_apply(mats_anti, win_grad, local_groups, per_group)
    gc4 = grad_conv.reshape(tiles, block, local_groups, per_group)
    wp4 = win_prod.reshape(tiles, width, local_groups, per_group)
    cross = jnp.einsum("kigc,kjgc->gij", gc4, wp4, preferred_element_type=jnp.float32)
    cross = jnp.pad(cross.reshape(local_groups, block * width), ((0, 0), (0, block)))
    diag = cross.reshape(local_groups, block, width + 1)[:, :, 1 : halo + 1].sum(axis=1)
    scale = (rows * ctx_count * per_group) ** (-0.5)
    local_filters = lax.psum(diag[:, ::-1], "ctx") * scale
    grad_filters = lax.all_gather(local_filters, "mp", axis=0, tiled=True)
    grad_query = (grad_mixed * mixed).astype(jnp.bfloat16)
    grad_key = (grad_product * value_act.astype(jnp.float32)).astype(jnp.bfloat16)
    grad_value = (grad_product * key_act.astype(jnp.float32)).astype(jnp.bfloat16)
    return (grad_query, grad_key, grad_value, grad_filters)


def solution(mesh):
    in_specs = (P("ctx", "mp"), P("mp", "ctx"), P("ctx", "mp"), P("ctx", "mp"), P("ctx", "mp"), P())
    out_specs = (P("ctx", "mp"), P("ctx", "mp"), P("ctx", "mp"), P())
    return jax.shard_map(body, mesh=mesh, in_specs=in_specs, out_specs=out_specs, check_vma=False)
```

profile of v0, /device:TPU:0, one launch (start us, length us, event | category | flops | bytes accessed | tf_op | source)
XLA Modules:
  0.0 473.6 jit_solution(11213987400638723255)
XLA Ops:
  8.7 67.1 %all-gather.3.cloned.1.call-done = bf16[192,8192]{1,0:T(8,128)(2,1)} async-done(((bf16[192,2048]{1,0:T(8,128)(2,1)}), bf16[192,8192]{1,0:T(8,128)(2,1)}) %all-gather.3.cloned.1.call-update) | async-done | bytes 3145744 | tf_op jit(solution)/shard_map/all_gather | solution.py:52
  75.8 161.4 %all-gather.5.cloned.1.call-done = bf16[2048,8192]{1,0:T(8,128)(2,1)} async-done(((bf16[2048,1024]{1,0:T(8,128)(2,1)}), bf16[2048,8192]{1,0:T(8,128)(2,1)}) %all-gather.5.cloned.1.call-update) | async-done | bytes 33554448 | tf_op jit(solution)/shard_map/all_gather | solution.py:51
  237.2 18.0 %multiply_convert_fusion = (bf16[192,2048]{1,0:T(8,128)(2,1)S(1)}, f32[192,2048]{1,0:T(8,128)}) fusion(bf16[192,2048]{1,0:T(8,128)(2,1)S(1)} %copy-done.8, bf16[192,8192]{1,0:T(8,128)(2,1)} %all-gather.3.cloned.1.call-done, bf16[2048,8192]{1,0:T(8,128)(2,1)} %all-gather.5.cloned.1.call-done), kind=kOutput, calls=%fused_computation.29 | convolution fusion | flops 6443630592 | bytes 39845888 | tf_op jit(solution)/shard_map/dot_general | solution.py:8
  260.1 6.0 %tile.21 = f32[128,12352]{0,1:T(8,128)} reshape(f32[128,64,193]{0,2,1:T(8,128)} %tile.20) | data formatting | bytes 12648448 | tf_op jit(solution)/shard_map/tile | solution.py:15
  266.1 4.7 slice.43
  270.8 9.1 %copy.54 = f32[128,64,192]{2,1,0:T(8,128)} copy(f32[128,64,192]{0,2,1:T(8,128)} %bitcast.66) | data formatting | bytes 12582912 | tf_op jit(solution)/shard_map/reshape | solution.py:16
  287.3 7.1 %fusion.4 = f32[128,3,16,64]{3,2,1,0:T(8,128)S(1)} fusion(f32[128,64,192]{2,1,0:T(8,128)} %copy.54, bf16[1,192,128,16]{1,3,0,2:T(8,128)(2,1)S(1)} %bitcast.76, bf16[1,192,128,16]{1,3,0,2:T(8,128)(2,1)S(1)} %bitcast.78, bf16[1,192,128,16]{1,3,0,2:T(8,128)(2,1)S(1)} %bitcast.68), kind=kOutput, calls=%fused_computation.5 | convolution fusion | flops 159645696 | bytes 10223616 | tf_op jit(solution)/shard_map/gij,kjgc->kigc/dot_general | solution.py:34
  294.3 4.2 add_bitcast_fusion
  298.6 3.7 copy.56
  302.3 5.9 %reshape.55 = f32[192,2048]{0,1:T(8,128)} reshape(f32[3,64,128,16]{1,0,3,2:T(4,128)} %copy.56) | data formatting | bytes 3145728 | tf_op jit(solution)/shard_map/reshape | solution.py:37
  308.2 3.8 fusion.10
  313.0 3.8 collective-permute-start
  320.0 6.0 %tile.9 = f32[128,12352]{0,1:T(8,128)} reshape(f32[128,64,193]{0,2,1:T(8,128)} %tile.8) | data formatting | bytes 12648448 | tf_op jit(solution)/shard_map/tile | solution.py:15
  326.1 4.7 slice.39
  330.8 9.0 %copy.43 = f32[128,64,192]{2,1,0:T(8,128)} copy(f32[128,64,192]{0,2,1:T(8,128)} %bitcast.67) | data formatting | bytes 12582912 | tf_op jit(solution)/shard_map/reshape | solution.py:16
  347.4 7.1 %fusion.1 = f32[128,3,16,64]{3,2,1,0:T(8,128)S(1)} fusion(f32[128,64,192]{2,1,0:T(8,128)} %copy.43, bf16[1,192,128,16]{1,3,0,2:T(8,128)(2,1)S(1)} %bitcast.62, bf16[1,192,128,16]{1,3,0,2:T(8,128)(2,1)S(1)} %bitcast.73, bf16[1,192,128,16]{1,3,0,2:T(8,128)(2,1)S(1)} %bitcast.70), kind=kOutput, calls=%fused_computation.3 | convolution fusion | flops 159645696 | bytes 10223616 | tf_op jit(solution)/shard_map/gij,kjgc->kigc/dot_general | solution.py:34
  356.0 3.7 copy.45
  359.8 5.8 %reshape.53 = f32[192,2048]{0,1:T(8,128)} reshape(f32[3,64,128,16]{1,0,3,2:T(4,128)} %copy.45) | data formatting | bytes 3145728 | tf_op jit(solution)/shard_map/reshape | solution.py:37
  368.3 6.2 %convolution_bitcast_fusion = f32[128,64,192]{2,1,0:T(8,128)} fusion(bf16[3,64,128,16]{1,0,3,2:T(4,128)(2,1)} %reshape.56, bf16[1,192,128,16]{1,3,0,2:T(8,128)(2,1)S(1)} %bitcast.64, bf16[1,192,128,16]{1,3,0,2:T(8,128)(2,1)S(1)} %bitcast.75, bf16[1,192,128,16]{1,3,0,2:T(8,128)(2,1)S(1)} %bitcast.72), kind=kOutput, calls=%fused_computation.11 | convolution fusion | flops 153354240 | bytes 9437184 | tf_op jit(solution)/shard_map/kigc,kjgc->gij/dot_general | solution.py:74
  374.5 8.6 %copy.59 = f32[128,64,192]{0,2,1:T(8,128)} copy(f32[128,64,192]{2,1,0:T(8,128)} %convolution_bitcast_fusion) | data formatting | bytes 12582912 | tf_op jit(solution)/shard_map/kigc,kjgc->gij/dot_general | solution.py:74
  383.1 4.8 %pad.4 = f32[128,12352]{0,1:T(8,128)} pad(f32[128,12288]{0,1:T(8,128)} %bitcast.65, f32[]{:T(128)} %constant.6.clone.1), padding=0_0x0_64 | pad | bytes 12615684 | tf_op jit(solution)/shard_map/jit(_pad)/pad | solution.py:75
  387.8 6.0 %reshape.58 = f32[128,64,193]{0,2,1:T(8,128)} reshape(f32[128,12352]{0,1:T(8,128)} %pad.4) | data formatting | bytes 12648448 | tf_op jit(solution)/shard_map/reshape | solution.py:76
  398.5 52.9 %all-reduce.3.cloned.1.call-done = f32[128,128]{0,1:T(8,128)} async-done(((f32[128,128]{0,1:T(8,128)}), f32[128,128]{0,1:T(8,128)}) %all-reduce.3.cloned.1.call-update) | async-done | bytes 65552 | tf_op jit(solution)/shard_map/psum | solution.py:78
  452.3 13.9 %all_gather.11 = f32[512,128]{0,1:T(8,128)S(1)} all-gather(f32[128,128]{0,1:T(8,128)S(1)} %broadcast_multiply_fusion), channel_id=1, replica_groups=mesh['ctx'=8,'mp'=4] {'mp'}, dimensions={0}, use_global_device_ids=true | all-gather | bytes 327680 | tf_op jit(solution)/shard_map/all_gather | solution.py:79
  (60 shorter events, 36.1 us)
Async XLA Ops:
  7.2 249.4 %copy-start = (f32[512,128]{1,0:T(8,128)S(1)}, f32[512,128]{1,0:T(8,128)}, u32[]{:S(2)}) copy-start(f32[512,128]{1,0:T(8,128)} %param.11) | copy-start | bytes 786436
  7.2 230.0 %copy-start.8 = (bf16[192,2048]{1,0:T(8,128)(2,1)S(1)}, bf16[192,2048]{1,0:T(8,128)(2,1)}, u32[]{:S(2)}) copy-start(bf16[192,2048]{1,0:T(8,128)(2,1)} %param.8) | copy-start | bytes 2359300
  7.2 68.6 %all-gather.3.cloned.1.call-start = ((), (), s32[]{:S(2)}) async-start(), calls=%async_computation | async-start | bytes 3932160 | tf_op jit(solution)/shard_map/all_gather | solution.py:52
  7.9 229.3 %all-gather.5.cloned.1.call-start = ((), (), s32[]{:S(2)}) async-start(), calls=%async_computation.1 | async-start | bytes 37748736 | tf_op jit(solution)/shard_map/all_gather | solution.py:51
  8.7 442.8 %all-reduce.3.cloned.1.call-start = ((), (), s32[]{:S(2)}) async-start(), calls=%async_computation.2 | async-start | bytes 131072 | tf_op jit(solution)/shard_map/psum | solution.py:78
  255.3 27.8 %collective-permute-start.1 = (bf16[128,2048]{1,0:T(8,128)(2,1)S(1)}, bf16[128,2048]{1,0:T(8,128)(2,1)}, u32[]{:S(2)}, u32[]{:S(2)}) collective-permute-start(bf16[128,2048]{1,0:T(8,128)(2,1)S(1)} %slice.40), channel_id=1, source_target_pairs={{4,0},{8,4},{12,8},{16,12},{20,16},{24,20},{28,24},{5,1},{9,5},{13... | collective-permute-start | bytes 1572872 | tf_op jit(solution)/shard_map/ppermute | solution.py:58
  270.8 9.1 %copy-start.6 = (bf16[192,2048]{1,0:T(8,128)(2,1)S(1)}, bf16[192,2048]{1,0:T(8,128)(2,1)}, u32[]{:S(2)}) copy-start(bf16[192,2048]{1,0:T(8,128)(2,1)} %param.9) | copy-start | bytes 2359300
  270.8 10.5 %copy-start.7 = (bf16[192,2048]{1,0:T(8,128)(2,1)S(1)}, bf16[192,2048]{1,0:T(8,128)(2,1)}, u32[]{:S(2)}) copy-start(bf16[192,2048]{1,0:T(8,128)(2,1)} %param.10) | copy-start | bytes 2359300
  302.3 5.9 %copy-start.3 = (bf16[192,2048]{0,1:T(8,128)(2,1)S(1)}, bf16[192,2048]{0,1:T(8,128)(2,1)}, u32[]{:S(2)}) copy-start(bf16[192,2048]{0,1:T(8,128)(2,1)} %copy.40) | copy-start | bytes 2359300
  313.0 32.4 %collective-permute-start = (bf16[128,2048]{0,1:T(8,128)(2,1)}, bf16[128,2048]{0,1:T(8,128)(2,1)}, u32[]{:S(2)}, u32[]{:S(2)}) collective-permute-start(bf16[128,2048]{0,1:T(8,128)(2,1)} %slice.36), channel_id=1, source_target_pairs={{0,4},{4,8},{8,12},{12,16},{16,20},{20,24},{24,28},{1,5},{5,9},{9,... | collective-permute-start | bytes 1572872 | tf_op jit(solution)/shard_map/ppermute | solution.py:57
  339.8 4.4 copy-start.4
  345.4 9.1 %slice-start = ((s8[8388608]{0:T(1024)(128)(4,1)}), s8[4194304]{0:T(1024)(128)(4,1)S(1)}, s32[]{:S(2)}) async-start(s8[8388608]{0:T(1024)(128)(4,1)} %bitcast.60), calls=%async_computation.3 | async-start | bytes 8388608
  347.4 7.2 %slice-start.1 = ((s8[8388608]{0:T(1024)(128)(4,1)}), s8[4194304]{0:T(1024)(128)(4,1)S(1)}, s32[]{:S(2)}) async-start(s8[8388608]{0:T(1024)(128)(4,1)} %bitcast.60), calls=%async_computation.4 | async-start | bytes 8388608
  393.9 3.6 copy-start.2
  393.9 3.6 copy-start.5
  393.9 73.2 %copy-start.1 = (f32[512,128]{1,0:T(8,128)S(1)}, f32[512,128]{1,0:T(8,128)}, u32[]{:S(2)}) copy-start(f32[512,128]{1,0:T(8,128)} %param.11) | copy-start | bytes 786436
Sparse Core Ops, SparseCore 0:
  9.6 66.1 all-gather.2
  77.7 159.4 all-gather.4
  397.5 53.8 all-reduce.2
where the time goes:
time: 475 us; the launch traced here: 474 us
  waiting for transfers between devices  283 us (60%)
  local copies, waits for them, and re-layouts  101 us (21%)
  matrix products  44.1 us (9%)
  between operations  14 us (3%)
  blocking collectives  13.9 us (3%)
  other arithmetic  12.9 us (3%)
  starting transfers between devices  5.24 us (1%)
    all_gather x1, waiting for transfers between devices, body(): panel = lax.all_gather(out_weight, 'ctx', axis=1, tiled=True)  161 us
    all_gather x1, waiting for transfers between devices, body(): lax.all_gather(cotangent, 'mp', axis=1, tiled=True)  67.1 us
    psum x1, waiting for transfers between devices, body(): local_filters = lax.psum(diag[:, ::-1], 'ctx') * scale  52.9 us
    dot_general x4, matrix products, filter_apply(): jnp.einsum('gij,kjgc->kigc', m, w4, preferred_element_type=jnp.float32)  19.9 us
    another operation x4, local copies, waits for them, and re-layouts, toeplitz(): flat = jnp.tile(seq, (1, block))[:, :block * width]  18.3 us
    reshape x2, local copies, waits for them, and re-layouts, toeplitz(): return flat.reshape(groups, block, width)  18.1 us
    dot_general x1, matrix products, contract(): lax.dot_general(left, right, (((1,), (1,)), ((), ())), preferred_element_...  18 us
    reshape x3, local copies, waits for them, and re-layouts, filter_apply(): return total.reshape(tiles * block, chans)  14.5 us
  transfers between devices with their start and end apart: 5, of which 3 were waited for; matrix products, arithmetic and copies ran while one was open for 12% of the time, Pallas kernels for 0%

commit v1 on v0

--- a/solution.py
+++ b/solution.py
@@ -75,7 +75,7 @@
     cross = jnp.pad(cross.reshape(local_groups, block * width), ((0, 0), (0, block)))
     diag = cross.reshape(local_groups, block, width + 1)[:, :, 1 : halo + 1].sum(axis=1)
     scale = (rows * ctx_count * per_group) ** (-0.5)
-    local_filters = lax.psum(diag[:, ::-1], "ctx") * scale
+    local_filters = jnp.sum(lax.all_gather(diag[:, ::-1], "ctx"), axis=0) * scale
     grad_filters = lax.all_gather(local_filters, "mp", axis=0, tiled=True)
     grad_query = (grad_mixed * mixed).astype(jnp.bfloat16)
     grad_key = (grad_product * value_act.astype(jnp.float32)).astype(jnp.bfloat16)

time: 475 us -> 435 us (0.916)
  waiting for transfers between devices: 283 us -> 230 us
  blocking collectives: 13.9 us -> 27 us
    psum x1 -> x0, waiting for transfers between devices: 52.9 us -> none  [body(): local_filters = lax.psum(diag[:, ::-1], 'ctx') * scale]
    all_gather x0 -> x1, blocking collectives: none -> 12.3 us  [body(): lax.all_gather(diag[:, ::-1], 'ctx')]
  transfers between devices with their start and end apart: 5 -> 4, of which waited for: 3 -> 2; matrix products, arithmetic and copies ran while one was open for 12% -> 13% of each run, Pallas kernels for 0% -> 0%
where the time goes in v1:
time: 435 us; the launch traced here: 434 us
  waiting for transfers between devices  230 us (53%)
  local copies, waits for them, and re-layouts  101 us (23%)
  matrix products  44.1 us (10%)
  blocking collectives  27 us (6%)
  between operations  14.3 us (3%)
  other arithmetic  12.2 us (3%)
  starting transfers between devices  5.2 us (1%)
    all_gather x1, waiting for transfers between devices, body(): panel = lax.all_gather(out_weight, 'ctx', axis=1, tiled=True)  161 us
    all_gather x1, waiting for transfers between devices, body(): lax.all_gather(cotangent, 'mp', axis=1, tiled=True)  67.1 us
    dot_general x4, matrix products, filter_apply(): jnp.einsum('gij,kjgc->kigc', m, w4, preferred_element_type=jnp.float32)  20 us
    another operation x4, local copies, waits for them, and re-layouts, toeplitz(): flat = jnp.tile(seq, (1, block))[:, :block * width]  18.3 us
    reshape x2, local copies, waits for them, and re-layouts, toeplitz(): return flat.reshape(groups, block, width)  18.3 us
    dot_general x1, matrix products, contract(): lax.dot_general(left, right, (((1,), (1,)), ((), ())), preferred_element_...  18 us
    all_gather x1, blocking collectives, body(): grad_filters = lax.all_gather(local_filters, 'mp', axis=0, tiled=True)  14.7 us
    reshape x3, local copies, waits for them, and re-layouts, filter_apply(): return total.reshape(tiles * block, chans)  14.5 us
  transfers between devices with their start and end apart: 4, of which 2 were waited for; matrix products, arithmetic and copies ran while one was open for 13% of the time, Pallas kernels for 0%

profile of v1, /device:TPU:0, one launch (start us, length us, event | category | flops | bytes accessed | tf_op | source)
XLA Modules:
  0.0 433.9 jit_solution(3029436258962600104)
XLA Ops:
  8.7 67.1 %all-gather.4.cloned.1.call-done = bf16[192,8192]{1,0:T(8,128)(2,1)} async-done(((bf16[192,2048]{1,0:T(8,128)(2,1)}), bf16[192,8192]{1,0:T(8,128)(2,1)}) %all-gather.4.cloned.1.call-update) | async-done | bytes 3145744 | tf_op jit(solution)/shard_map/all_gather | solution.py:52
  75.8 161.4 %all-gather.6.cloned.1.call-done = bf16[2048,8192]{1,0:T(8,128)(2,1)} async-done(((bf16[2048,1024]{1,0:T(8,128)(2,1)}), bf16[2048,8192]{1,0:T(8,128)(2,1)}) %all-gather.6.cloned.1.call-update) | async-done | bytes 33554448 | tf_op jit(solution)/shard_map/all_gather | solution.py:51
  237.2 18.0 %multiply_convert_fusion = (bf16[192,2048]{1,0:T(8,128)(2,1)S(1)}, f32[192,2048]{1,0:T(8,128)}) fusion(bf16[192,2048]{1,0:T(8,128)(2,1)S(1)} %copy-done.8, bf16[192,8192]{1,0:T(8,128)(2,1)} %all-gather.4.cloned.1.call-done, bf16[2048,8192]{1,0:T(8,128)(2,1)} %all-gather.6.cloned.1.call-done), kind=kOutput, calls=%fused_computation.29 | convolution fusion | flops 6443630592 | bytes 39845888 | tf_op jit(solution)/shard_map/dot_general | solution.py:8
  260.1 6.0 %tile.21 = f32[128,12352]{0,1:T(8,128)} reshape(f32[128,64,193]{0,2,1:T(8,128)} %tile.20) | data formatting | bytes 12648448 | tf_op jit(solution)/shard_map/tile | solution.py:15
  266.1 4.7 %slice.43 = f32[128,12288]{0,1:T(8,128)} slice(f32[128,12352]{0,1:T(8,128)} %tile.21), slice={[0:128], [0:12288]} | slice | bytes 12582912 | tf_op jit(solution)/shard_map/slice | solution.py:15
  270.8 9.2 %copy.76 = f32[128,64,192]{2,1,0:T(8,128)} copy(f32[128,64,192]{0,2,1:T(8,128)} %bitcast.71) | data formatting | bytes 12582912 | tf_op jit(solution)/shard_map/reshape | solution.py:16
  287.4 7.1 %fusion.4 = f32[128,3,16,64]{3,2,1,0:T(8,128)S(1)} fusion(f32[128,64,192]{2,1,0:T(8,128)} %copy.76, bf16[1,192,128,16]{1,3,0,2:T(8,128)(2,1)S(1)} %bitcast.81, bf16[1,192,128,16]{1,3,0,2:T(8,128)(2,1)S(1)} %bitcast.83, bf16[1,192,128,16]{1,3,0,2:T(8,128)(2,1)S(1)} %bitcast.73), kind=kOutput, calls=%fused_computation.5 | convolution fusion | flops 159645696 | bytes 10223616 | tf_op jit(solution)/shard_map/gij,kjgc->kigc/dot_general | solution.py:34
  294.4 4.2 add_bitcast_fusion
  298.7 3.7 copy.78
  302.4 5.9 %reshape.55 = f32[192,2048]{0,1:T(8,128)} reshape(f32[3,64,128,16]{1,0,3,2:T(4,128)} %copy.78) | data formatting | bytes 3145728 | tf_op jit(solution)/shard_map/reshape | solution.py:37
  308.3 3.8 fusion.10
  313.1 3.8 collective-permute-start
  320.1 6.0 %tile.9 = f32[128,12352]{0,1:T(8,128)} reshape(f32[128,64,193]{0,2,1:T(8,128)} %tile.8) | data formatting | bytes 12648448 | tf_op jit(solution)/shard_map/tile | solution.py:15
  326.1 4.7 %slice.39 = f32[128,12288]{0,1:T(8,128)} slice(f32[128,12352]{0,1:T(8,128)} %tile.9), slice={[0:128], [0:12288]} | slice | bytes 12582912 | tf_op jit(solution)/shard_map/slice | solution.py:15
  330.9 9.1 %copy.65 = f32[128,64,192]{2,1,0:T(8,128)} copy(f32[128,64,192]{0,2,1:T(8,128)} %bitcast.72) | data formatting | bytes 12582912 | tf_op jit(solution)/shard_map/reshape | solution.py:16
  347.6 7.1 %fusion.1 = f32[128,3,16,64]{3,2,1,0:T(8,128)S(1)} fusion(f32[128,64,192]{2,1,0:T(8,128)} %copy.65, bf16[1,192,128,16]{1,3,0,2:T(8,128)(2,1)S(1)} %bitcast.67, bf16[1,192,128,16]{1,3,0,2:T(8,128)(2,1)S(1)} %bitcast.78, bf16[1,192,128,16]{1,3,0,2:T(8,128)(2,1)S(1)} %bitcast.75), kind=kOutput, calls=%fused_computation.3 | convolution fusion | flops 159645696 | bytes 10223616 | tf_op jit(solution)/shard_map/gij,kjgc->kigc/dot_general | solution.py:34
  356.2 3.7 copy.67
  360.0 5.8 %reshape.53 = f32[192,2048]{0,1:T(8,128)} reshape(f32[3,64,128,16]{1,0,3,2:T(4,128)} %copy.67) | data formatting | bytes 3145728 | tf_op jit(solution)/shard_map/reshape | solution.py:37
  368.6 6.1 %convolution_bitcast_fusion = f32[128,64,192]{2,1,0:T(8,128)} fusion(bf16[3,64,128,16]{1,0,3,2:T(4,128)(2,1)} %reshape.56, bf16[1,192,128,16]{1,3,0,2:T(8,128)(2,1)S(1)} %bitcast.69, bf16[1,192,128,16]{1,3,0,2:T(8,128)(2,1)S(1)} %bitcast.80, bf16[1,192,128,16]{1,3,0,2:T(8,128)(2,1)S(1)} %bitcast.77), kind=kOutput, calls=%fused_computation.11 | convolution fusion | flops 153354240 | bytes 9437184 | tf_op jit(solution)/shard_map/kigc,kjgc->gij/dot_general | solution.py:74
  374.7 8.6 %copy.81 = f32[128,64,192]{0,2,1:T(8,128)} copy(f32[128,64,192]{2,1,0:T(8,128)} %convolution_bitcast_fusion) | data formatting | bytes 12582912 | tf_op jit(solution)/shard_map/kigc,kjgc->gij/dot_general | solution.py:74
  383.3 4.7 %pad.4 = f32[128,12352]{0,1:T(8,128)} pad(f32[128,12288]{0,1:T(8,128)} %bitcast.70, f32[]{:T(128)} %constant.6.clone.1), padding=0_0x0_64 | pad | bytes 12615684 | tf_op jit(solution)/shard_map/jit(_pad)/pad | solution.py:75
  388.1 6.0 %reshape.58 = f32[128,64,193]{0,2,1:T(8,128)} reshape(f32[128,12352]{0,1:T(8,128)} %pad.4) | data formatting | bytes 12648448 | tf_op jit(solution)/shard_map/reshape | solution.py:76
  397.0 12.3 %all-gather = f32[1024,128]{0,1:T(8,128)S(1)} all-gather(f32[128,128]{0,1:T(8,128)S(1)} %rev.7), channel_id=2, replica_groups=mesh['ctx'=8,'mp'=4] {'ctx'}, dimensions={0}, use_global_device_ids=true | all-gather | bytes 589824 | tf_op jit(solution)/shard_map/all_gather | solution.py:78
  409.6 14.7 %all_gather.19 = f32[512,128]{0,1:T(8,128)} all-gather(f32[128,128]{0,1:T(8,128)S(1)} %broadcast_multiply_fusion), channel_id=1, replica_groups=mesh['ctx'=8,'mp'=4] {'mp'}, dimensions={0}, use_global_device_ids=true | all-gather | bytes 327680 | tf_op jit(solution)/shard_map/all_gather | solution.py:79
  (60 shorter events, 35.8 us)
Async XLA Ops:
  7.2 249.4 %copy-start = (f32[512,128]{1,0:T(8,128)S(1)}, f32[512,128]{1,0:T(8,128)}, u32[]{:S(2)}) copy-start(f32[512,128]{1,0:T(8,128)} %param.11) | copy-start | bytes 786436
  7.2 230.0 %copy-start.8 = (bf16[192,2048]{1,0:T(8,128)(2,1)S(1)}, bf16[192,2048]{1,0:T(8,128)(2,1)}, u32[]{:S(2)}) copy-start(bf16[192,2048]{1,0:T(8,128)(2,1)} %param.8) | copy-start | bytes 2359300
  7.2 68.6 %all-gather.4.cloned.1.call-start = ((), (), s32[]{:S(2)}) async-start(), calls=%async_computation | async-start | bytes 3932160 | tf_op jit(solution)/shard_map/all_gather | solution.py:52
  7.9 229.3 %all-gather.6.cloned.1.call-start = ((), (), s32[]{:S(2)}) async-start(), calls=%async_computation.1 | async-start | bytes 37748736 | tf_op jit(solution)/shard_map/all_gather | solution.py:51
  255.3 27.9 %collective-permute-start.1 = (bf16[128,2048]{1,0:T(8,128)(2,1)S(1)}, bf16[128,2048]{1,0:T(8,128)(2,1)}, u32[]{:S(2)}, u32[]{:S(2)}) collective-permute-start(bf16[128,2048]{1,0:T(8,128)(2,1)S(1)} %slice.40), channel_id=1, source_target_pairs={{4,0},{8,4},{12,8},{16,12},{20,16},{24,20},{28,24},{5,1},{9,5},{13... | collective-permute-start | bytes 1572872 | tf_op jit(solution)/shard_map/ppermute | solution.py:58
  270.8 9.2 %copy-start.6 = (bf16[192,2048]{1,0:T(8,128)(2,1)S(1)}, bf16[192,2048]{1,0:T(8,128)(2,1)}, u32[]{:S(2)}) copy-start(bf16[192,2048]{1,0:T(8,128)(2,1)} %param.9) | copy-start | bytes 2359300
  270.8 10.6 %copy-start.7 = (bf16[192,2048]{1,0:T(8,128)(2,1)S(1)}, bf16[192,2048]{1,0:T(8,128)(2,1)}, u32[]{:S(2)}) copy-start(bf16[192,2048]{1,0:T(8,128)(2,1)} %param.10) | copy-start | bytes 2359300
  302.4 5.9 %copy-start.3 = (bf16[192,2048]{0,1:T(8,128)(2,1)S(1)}, bf16[192,2048]{0,1:T(8,128)(2,1)}, u32[]{:S(2)}) copy-start(bf16[192,2048]{0,1:T(8,128)(2,1)} %copy.62) | copy-start | bytes 2359300
  313.1 32.5 %collective-permute-start = (bf16[128,2048]{0,1:T(8,128)(2,1)}, bf16[128,2048]{0,1:T(8,128)(2,1)}, u32[]{:S(2)}, u32[]{:S(2)}) collective-permute-start(bf16[128,2048]{0,1:T(8,128)(2,1)} %slice.36), channel_id=1, source_target_pairs={{0,4},{4,8},{8,12},{12,16},{16,20},{20,24},{24,28},{1,5},{5,9},{9,... | collective-permute-start | bytes 1572872 | tf_op jit(solution)/shard_map/ppermute | solution.py:57
  339.9 4.4 %copy-start.4 = (bf16[192,2048]{0,1:T(8,128)(2,1)S(1)}, bf16[192,2048]{0,1:T(8,128)(2,1)}, u32[]{:S(2)}) copy-start(bf16[192,2048]{0,1:T(8,128)(2,1)} %get-tuple-element.16) | copy-start | bytes 2359300
  345.5 9.1 %slice-start = ((s8[8388608]{0:T(1024)(128)(4,1)}), s8[4194304]{0:T(1024)(128)(4,1)S(1)}, s32[]{:S(2)}) async-start(s8[8388608]{0:T(1024)(128)(4,1)} %bitcast.65), calls=%async_computation.2 | async-start | bytes 8388608
  347.5 7.2 %slice-start.1 = ((s8[8388608]{0:T(1024)(128)(4,1)}), s8[4194304]{0:T(1024)(128)(4,1)S(1)}, s32[]{:S(2)}) async-start(s8[8388608]{0:T(1024)(128)(4,1)} %bitcast.65), calls=%async_computation.3 | async-start | bytes 8388608
  394.1 31.9 %copy-start.2 = (f32[192,2048]{1,0:T(8,128)S(1)}, f32[192,2048]{1,0:T(8,128)}, u32[]{:S(2)}) copy-start(f32[192,2048]{1,0:T(8,128)} %copy.68) | copy-start | bytes 4718596
  394.1 31.9 %copy-start.5 = (f32[192,2048]{1,0:T(8,128)S(1)}, f32[192,2048]{1,0:T(8,128)}, u32[]{:S(2)}) copy-start(f32[192,2048]{1,0:T(8,128)} %get-tuple-element.26) | copy-start | bytes 4718596
  409.3 17.8 %copy-start.1 = (f32[512,128]{1,0:T(8,128)S(1)}, f32[512,128]{1,0:T(8,128)}, u32[]{:S(2)}) copy-start(f32[512,128]{1,0:T(8,128)} %param.11) | copy-start | bytes 786436
Sparse Core Ops, SparseCore 0:
  9.6 66.1 all-gather.3
  77.7 159.4 all-gather.5
